TPU v7x, 512 devices: a whole 4x8x8 slice. The times are simulated.
512 devices in a mesh: doc: 16 (over z_lo, y), label: 32 (over x, z_hi, core).
Axes of the slice: x: 4, y: 8, z: 8 (z_hi: 4, z_lo: 2; z = z_hi * 2 + z_lo), core: 2. Of those that a mesh axis runs over, the one named last changes fastest.
Arguments:
- doc_embed: bfloat16 [16384, 768], P(('doc', 'label')), may hold values from -0.59765625 to 0.59765625
- classifier: bfloat16 [32768, 768], P('label'), may hold values from -4.28125 to 4.28125
- centroids: bfloat16 [256, 768], P('doc'), may hold values from -4.28125 to 4.28125
- shortlist: int32 [16384, 32], P(('doc', 'label')), may hold values from 0 to 255, all different within a row
- positives: int32 [16384, 4], P(('doc', 'label')), may hold values from 0 to 4095
Outputs:
- grad_classifier: bfloat16 [32768, 768], P('label')
- grad_centroids: float32 [256, 768], P('doc')
- grad_docs: bfloat16 [16384, 768], P(('doc', 'label'))
Inputs may be any that keep to these rules, and one draw needn't show every extreme that they name: `shortlist`: each row names 32 different clusters; every cluster is named by some row.
All inputs are finite; a program needn't handle non-finite values.
Results may differ from a plain program's by a relative error of at most 0.015.
Values may be sent and summed in bfloat16 or wider, within the bound.
No kernel may reach another device: no remote copies, remote signals or barrier semaphores. Data moves between devices by JAX's collectives and lax.ppermute only.
A program may use at most 64 MiB of HBM per device.

v0:
```python
import jax
import jax.numpy as jnp
from jax import lax
from jax.sharding import PartitionSpec as P


CLS = 128
LOSS_WEIGHT = 0.125


def step(doc_embed, classifier, centroids, shortlist, positives):
    n_doc = lax.axis_size("doc")
    labels_dev, width = classifier.shape
    cl_here = labels_dev // CLS
    per_doc = centroids.shape[0]
    docs_dev, short = shortlist.shape
    n_pos = positives.shape[1]
    label_index = lax.axis_index("label")
    cluster_base = label_index * cl_here

    n_label = lax.axis_size("label")
    pos_cluster = jnp.take_along_axis(shortlist, positives // CLS, axis=1)
    ints = jnp.concatenate([shortlist, pos_cluster, positives % CLS], axis=1)
    ints_rows = lax.all_to_all(
        jnp.broadcast_to(ints[None], (n_label,) + ints.shape).reshape(n_label * docs_dev, -1),
        "label", 0, 0, tiled=True,
    )
    all_cent = lax.all_to_all(
        jnp.broadcast_to(centroids[None], (n_doc,) + centroids.shape).reshape(n_doc * per_doc, width),
        "doc", 0, 0, tiled=True,
    )
    n_clusters = all_cent.shape[0]
    short_rows = ints_rows[:, :short]
    pcl_rows = ints_rows[:, short : short + n_pos]
    pos_local = pcl_rows * CLS + ints_rows[:, short + n_pos :] - cluster_base * CLS
    local_clusters = cluster_base + jnp.arange(cl_here, dtype=jnp.int32)
    member = jnp.any(short_rows[:, :, None] == local_clusters[None, None, :], axis=1)
    member = member.astype(jnp.float32)

    rows = lax.all_gather(doc_embed, "label", axis=0, tiled=True)
    rows, all_cent, member, pos_local, pcl_rows = lax.optimization_barrier(
        (rows, all_cent, member, pos_local, pcl_rows)
    )

    logits = jnp.einsum("nd,ld->nl", rows, classifier, preferred_element_type=jnp.float32)
    label_ids = jnp.arange(labels_dev, dtype=jnp.int32).reshape(1, cl_here, CLS)
    target = pos_local[:, 0, None, None] == label_ids
    for p in range(1, n_pos):
        target = target | (pos_local[:, p, None, None] == label_ids)
    grad = (
        LOSS_WEIGHT
        * (jax.nn.sigmoid(logits.reshape(-1, cl_here, CLS)) - target.astype(jnp.float32))
        * member[:, :, None]
    ).astype(jnp.bfloat16).reshape(-1, labels_dev)

    docs_part = jnp.dot(grad, classifier, preferred_element_type=jnp.float32).astype(jnp.bfloat16)
    docs_sum = lax.psum_scatter(docs_part, "label", scatter_dimension=0, tiled=True)

    meta_logits = jnp.einsum("nd,cd->nc", rows, all_cent, preferred_element_type=jnp.float32)
    cluster_ids = jnp.arange(n_clusters, dtype=jnp.int32)
    meta_target = pcl_rows[:, 0, None] == cluster_ids[None, :]
    for p in range(1, n_pos):
        meta_target = meta_target | (pcl_rows[:, p, None] == cluster_ids[None, :])
    meta_grad = (
        LOSS_WEIGHT * (jax.nn.sigmoid(meta_logits) - meta_target.astype(jnp.float32))
    ).astype(jnp.bfloat16)
    cent_part = jnp.einsum("nc,nd->cd", meta_grad, rows, preferred_element_type=jnp.float32)
    half = per_doc // 2
    parity = label_index % 2
    cent_mine = lax.dynamic_slice_in_dim(
        cent_part.reshape(n_doc, 2, half, width), parity, 1, 1
    ).astype(jnp.bfloat16)

    class_part = jnp.einsum("nl,nd->ld", grad, rows, preferred_element_type=jnp.float32).astype(jnp.bfloat16)
    sub = labels_dev // n_doc
    send = jnp.concatenate(
        [class_part.reshape(n_doc, sub, width), cent_mine.reshape(n_doc, half, width)],
        axis=1,
    ).reshape(n_doc * (sub + half), width)
    recv = lax.all_to_all(send, "doc", 0, 0, tiled=True)
    recv = recv.reshape(n_doc, sub + half, width)
    class_sum = jnp.sum(recv[:, :sub].astype(jnp.float32), axis=0).astype(jnp.bfloat16)
    cent_sum = jnp.sum(recv[:, sub:].astype(jnp.float32), axis=0)
    n_label = lax.axis_size("label")
    cent_other = lax.ppermute(cent_sum, "label", [(i, i ^ 1) for i in range(n_label)])
    grad_centroids = jnp.where(
        parity == 0,
        jnp.concatenate([cent_sum, cent_other], axis=0),
        jnp.concatenate([cent_other, cent_sum], axis=0),
    )
    spread = jnp.broadcast_to(class_sum[None], (n_doc, sub, width)).reshape(n_doc * sub, width)
    gathered_class = lax.all_to_all(spread, "doc", 0, 0, tiled=True)
    grad_classifier = jnp.where(parity >= 0, gathered_class, jnp.zeros_like(gathered_class))

    local_meta = lax.dynamic_slice_in_dim(meta_grad, label_index * docs_dev, docs_dev, 0)
    meta_term = jnp.dot(local_meta, all_cent, preferred_element_type=jnp.float32)
    grad_docs = (docs_sum.astype(jnp.float32) + meta_term).astype(jnp.bfloat16)
    return (grad_classifier, grad_centroids, grad_docs)


def solution(mesh):
    in_specs = (
        P(("doc", "label"), None),
        P("label", None),
        P("doc", None),
        P(("doc", "label"), None),
        P(("doc", "label"), None),
    )
    out_specs = (P("label", None), P("doc", None), P(("doc", "label"), None))
    return jax.shard_map(step, mesh=mesh, in_specs=in_specs, out_specs=out_specs, check_vma=False)
```

profile of v0, /device:TPU:8, one launch (start us, length us, event | category | flops | bytes accessed | tf_op | source)
XLA Modules:
  0.0 254.1 jit_solution(18400112912999031992)
XLA Ops:
  7.2 0.7 all-gather.2.cloned.1.call-update
  7.9 0.7 bitcast_or_fusion
  8.9 1.3 gather_fusion
  10.7 1.1 reshape.131
  11.8 13.2 %all-to-all-start.1 = ((s32[32,1,1280]{2,1,0:T(1,128)}), s32[32,1,1280]{2,1,0:T(1,128)S(1)}, u32[]{:S(2)}, u32[]{:S(2)}) async-start(s32[32,1,1280]{2,1,0:T(1,128)} %reshape.131), calls=%async_computation.1 | async-start | bytes 327680 | tf_op jit(solution)/shard_map/all_to_all | solution.py:24
  24.9 11.9 %all-to-all-done.1 = s32[32,1,1280]{2,1,0:T(1,128)S(1)} async-done(((s32[32,1,1280]{2,1,0:T(1,128)}), s32[32,1,1280]{2,1,0:T(1,128)S(1)}, u32[]{:S(2)}, u32[]{:S(2)}) %all-to-all-start.1) | async-done | bytes 163872 | tf_op jit(solution)/shard_map/all_to_all | solution.py:24
  36.8 0.8 broadcast_in_dim.12
  37.6 7.8 %all-to-all-start = ((bf16[16,16,768]{2,1,0:T(8,128)(2,1)}), bf16[16,16,768]{2,1,0:T(8,128)(2,1)S(1)}, u32[]{:S(2)}, u32[]{:S(2)}) async-start(bf16[16,16,768]{2,1,0:T(8,128)(2,1)} %broadcast_in_dim.12), calls=%async_computation | async-start | bytes 786432 | tf_op jit(solution)/shard_map/all_to_all | solution.py:28
  47.1 1.0 reduce.1
  49.4 0.8 compare_reduce_fusion
  50.3 8.5 %all-to-all-done = bf16[16,16,768]{2,1,0:T(8,128)(2,1)S(1)} async-done(((bf16[16,16,768]{2,1,0:T(8,128)(2,1)}), bf16[16,16,768]{2,1,0:T(8,128)(2,1)S(1)}, u32[]{:S(2)}, u32[]{:S(2)}) %all-to-all-start) | async-done | bytes 393248 | tf_op jit(solution)/shard_map/all_to_all | solution.py:28
  58.8 15.8 %all-gather.2.cloned.1.call-done = bf16[1024,768]{1,0:T(8,128)(2,1)} async-done(((bf16[32,768]{1,0:T(8,128)(2,1)}), bf16[1024,768]{1,0:T(8,128)(2,1)}) %all-gather.2.cloned.1.call-update) | async-done | bytes 1572880 | tf_op jit(solution)/shard_map/all_gather | solution.py:40
  74.9 1.1 mul.44
  76.3 3.6 %fusion = bf16[1024,1024]{1,0:T(8,128)(2,1)S(1)} fusion(f32[128,8,8,128]{3,2,1,0:T(8,128)S(1)} %bitcast.44, bf16[1024,768]{1,0:T(8,128)(2,1)S(1)} %copy-done.2, bf16[1024,768]{1,0:T(8,128)(2,1)S(1)} %copy-done, s32[1024]{0:T(1024)S(1)} %copy-done.7, s32[1024]{0:T(1024)S(1)} %bitcast.51, s32[1024]{0:T(1024)S(1)} %bitcast.52, s32[1024]{0:T(1024)S(1)} %bitcast.53, ...), kind=kOutput, calls=%fused_computation.2 | convolution fusion | flops 1625292800 | bytes 9457664 | tf_op jit(solution)/shard_map/nd,ld->nl/dot_general | solution.py:45
  79.9 1.9 convolution_convert_fusion.1
  81.8 1.2 fusion.6
  84.0 50.3 %all_to_all.30 = bf16[16,72,768]{2,1,0:T(8,128)(2,1)S(1)} all-to-all(bf16[16,72,768]{2,1,0:T(8,128)(2,1)S(1)} %pad_maximum_fusion), channel_id=1, replica_groups=mesh['doc'=16,'label'=32] {'doc'}, dimensions={0} | all-to-all | bytes 3538944 | tf_op jit(solution)/shard_map/all_to_all | solution.py:80
  134.5 1.3 broadcast_in_dim.15
  135.8 4.3 %all-to-all-start.3 = ((bf16[16,64,768]{2,1,0:T(8,128)(2,1)}), bf16[16,64,768]{2,1,0:T(8,128)(2,1)}, u32[]{:S(2)}, u32[]{:S(2)}) async-start(bf16[16,64,768]{2,1,0:T(8,128)(2,1)} %broadcast_in_dim.15), calls=%async_computation.3 | async-start | bytes 3145728 | tf_op jit(solution)/shard_map/all_to_all | solution.py:92
  140.2 4.5 %convolution_convert_fusion = bf16[1024,768]{1,0:T(8,128)(2,1)} fusion(bf16[1024,1024]{1,0:T(8,128)(2,1)} %copy-done.8, bf16[1024,768]{1,0:T(8,128)(2,1)S(1)} %copy-done), kind=kOutput, calls=%fused_computation.4 | convolution fusion | flops 1611399168 | bytes 5242880 | tf_op jit(solution)/shard_map/dot_general | solution.py:56
  144.8 1.9 collective-permute-start
  146.7 95.5 %reduce-scatter.2.cloned.1.call-done = bf16[32,768]{1,0:T(8,128)(2,1)} async-done(((bf16[1024,768]{1,0:T(8,128)(2,1)}), bf16[32,768]{1,0:T(8,128)(2,1)}) %reduce-scatter.2.cloned.1.call-update) | async-done | bytes 49168 | tf_op jit(solution)/shard_map/reduce_scatter | solution.py:57
  242.1 1.8 fusion.7
  244.6 2.7 %broadcast_select_fusion = bf16[16,64,768]{2,1,0:T(8,128)(2,1)} fusion(bf16[16,64,768]{2,1,0:T(8,128)(2,1)} %all-to-all-done.3, pred[]{:T(512)S(6)} %ge.10), kind=kLoop, calls=%fused_computation.7 | loop fusion | flops 786432 | bytes 3145729 | tf_op jit(solution)/shard_map/jit(_where)/select_n | solution.py:93
  (52 shorter events, 6.1 us)
Async XLA Ops:
  7.2 68.9 %copy-start = (bf16[1024,768]{1,0:T(8,128)(2,1)S(1)}, bf16[1024,768]{1,0:T(8,128)(2,1)}, u32[]{:S(2)}) copy-start(bf16[1024,768]{1,0:T(8,128)(2,1)} %param.6) | copy-start | bytes 4718596
  7.2 1.6 copy-start.1
  7.2 67.4 %all-gather.2.cloned.1.call-start = ((), (), s32[]{:S(2)}) async-start(), calls=%async_computation.5 | async-start | bytes 1622016 | tf_op jit(solution)/shard_map/all_gather | solution.py:40
  8.8 1.5 copy-start.6
  8.8 28.0 %copy-start.5 = (bf16[16,768]{1,0:T(8,128)(2,1)S(1)}, bf16[16,768]{1,0:T(8,128)(2,1)}, u32[]{:S(2)}) copy-start(bf16[16,768]{1,0:T(8,128)(2,1)} %param.7) | copy-start | bytes 73732
  11.8 25.0 %all-to-all-start.1 = ((s32[32,1,1280]{2,1,0:T(1,128)}), s32[32,1,1280]{2,1,0:T(1,128)S(1)}, u32[]{:S(2)}, u32[]{:S(2)}) async-start(s32[32,1,1280]{2,1,0:T(1,128)} %reshape.131), calls=%async_computation.1 | async-start | bytes 327680 | tf_op jit(solution)/shard_map/all_to_all | solution.py:24
  37.6 21.2 %all-to-all-start = ((bf16[16,16,768]{2,1,0:T(8,128)(2,1)}), bf16[16,16,768]{2,1,0:T(8,128)(2,1)S(1)}, u32[]{:S(2)}, u32[]{:S(2)}) async-start(bf16[16,16,768]{2,1,0:T(8,128)(2,1)} %broadcast_in_dim.12), calls=%async_computation | async-start | bytes 786432 | tf_op jit(solution)/shard_map/all_to_all | solution.py:28
  58.8 23.0 %copy-start.3 = (bf16[16,16,768]{2,1,0:T(8,128)(2,1)}, bf16[16,16,768]{2,1,0:T(8,128)(2,1)S(1)}, u32[]{:S(2)}) copy-start(bf16[16,16,768]{2,1,0:T(8,128)(2,1)S(1)} %all-to-all-done) | copy-start | bytes 1179652
  74.9 1.4 copy-start.2
  74.9 1.4 copy-start.7
  79.9 1.9 copy-start.8
  83.0 0.8 copy-start.4
  135.8 108.8 %all-to-all-start.3 = ((bf16[16,64,768]{2,1,0:T(8,128)(2,1)}), bf16[16,64,768]{2,1,0:T(8,128)(2,1)}, u32[]{:S(2)}, u32[]{:S(2)}) async-start(bf16[16,64,768]{2,1,0:T(8,128)(2,1)} %broadcast_in_dim.15), calls=%async_computation.3 | async-start | bytes 3145728 | tf_op jit(solution)/shard_map/all_to_all | solution.py:92
  140.1 102.0 %reduce-scatter.2.cloned.1.call-start = ((), (), s32[]{:S(2)}) async-start(), calls=%async_computation.6 | async-start | bytes 1622016 | tf_op jit(solution)/shard_map/reduce_scatter | solution.py:57
  144.8 99.2 %collective-permute-start = (f32[8,768]{1,0:T(8,128)S(1)}, f32[8,768]{1,0:T(8,128)S(1)}, u32[]{:S(2)}, u32[]{:S(2)}) collective-permute-start(f32[8,768]{1,0:T(8,128)S(1)} %convert_reduce_fusion), channel_id=1, source_target_pairs={{0,1},{1,0},{2,3},{3,2},{4,5},{5,4},{6,7},{7,6},{8,9},{9,8},{10,11... | collective-permute-start | bytes 73736 | tf_op jit(solution)/shard_map/ppermute | solution.py:85
Sparse Core Ops, SparseCore 0:
  11.1 63.4 all-gather.1
  145.3 96.7 reduce-scatter.1
where the time goes:
time: 255 us; the launch traced here: 254 us
  waiting for transfers between devices  132 us (52%)
  blocking collectives  50.3 us (20%)
  starting transfers between devices  27.3 us (11%)
  between operations  14.3 us (6%)
  matrix products  13.6 us (5%)
  local copies, waits for them, and re-layouts  8.73 us (3%)
  other arithmetic  7.47 us (3%)
    reduce_scatter x1, waiting for transfers between devices, step(): lax.psum_scatter(docs_part, 'label', scatter_dimension=0, tiled=True)  95.5 us
    all_to_all x1, blocking collectives, step(): recv = lax.all_to_all(send, 'doc', 0, 0, tiled=True)  50.3 us
    all_gather x1, waiting for transfers between devices, step(): rows = lax.all_gather(doc_embed, 'label', axis=0, tiled=True)  15.8 us
    all_to_all x1, starting transfers between devices, step(): lax.all_to_all(jnp.broadcast_to(ints[None], (n_label,) + ints.shape).resh...  13.2 us
    all_to_all x1, waiting for transfers between devices, step(): lax.all_to_all(jnp.broadcast_to(ints[None], (n_label,) + ints.shape).resh...  11.9 us
    all_to_all x1, waiting for transfers between devices, step(): lax.all_to_all(jnp.broadcast_to(centroids[None], (n_doc,) + centroids.sha...  8.49 us
    all_to_all x1, starting transfers between devices, step(): lax.all_to_all(jnp.broadcast_to(centroids[None], (n_doc,) + centroids.sha...  7.82 us
  transfers between devices with their start and end apart: 6, of which 4 were waited for; matrix products, arithmetic and copies ran while one was open for 6% of the time, Pallas kernels for 0%

commit v1 on v0

--- a/solution.py
+++ b/solution.py
@@ -35,7 +35,7 @@
     pos_local = pcl_rows * CLS + ints_rows[:, short + n_pos :] - cluster_base * CLS
     local_clusters = cluster_base + jnp.arange(cl_here, dtype=jnp.int32)
     member = jnp.any(short_rows[:, :, None] == local_clusters[None, None, :], axis=1)
-    member = member.astype(jnp.float32)
+    member = member.astype(jnp.bfloat16)
 
     rows = lax.all_gather(doc_embed, "label", axis=0, tiled=True)
     rows, all_cent, member, pos_local, pcl_rows = lax.optimization_barrier(
@@ -48,10 +48,10 @@
     for p in range(1, n_pos):
         target = target | (pos_local[:, p, None, None] == label_ids)
     grad = (
-        LOSS_WEIGHT
-        * (jax.nn.sigmoid(logits.reshape(-1, cl_here, CLS)) - target.astype(jnp.float32))
+        (LOSS_WEIGHT * (jax.nn.sigmoid(logits.reshape(-1, cl_here, CLS)) - target.astype(jnp.float32)))
+        .astype(jnp.bfloat16)
         * member[:, :, None]
-    ).astype(jnp.bfloat16).reshape(-1, labels_dev)
+    ).reshape(-1, labels_dev)
 
     docs_part = jnp.dot(grad, classifier, preferred_element_type=jnp.float32).astype(jnp.bfloat16)
     docs_sum = lax.psum_scatter(docs_part, "label", scatter_dimension=0, tiled=True)

time: 255 us -> 260 us (1.020)
  local copies, waits for them, and re-layouts: 8.73 us -> 13.6 us
  transfers between devices with their start and end apart: 6 -> 6, of which waited for: 4 -> 4; matrix products, arithmetic and copies ran while one was open for 6% -> 7% of each run, Pallas kernels for 0% -> 0%
where the time goes in v1:
time: 260 us; the launch traced here: 259 us
  waiting for transfers between devices  131 us (50%)
  blocking collectives  50.3 us (19%)
  starting transfers between devices  27.3 us (10%)
  between operations  14.3 us (6%)
  local copies, waits for them, and re-layouts  13.6 us (5%)
  matrix products  13.6 us (5%)
  other arithmetic  8.66 us (3%)
    reduce_scatter x1, waiting for transfers between devices, step(): lax.psum_scatter(docs_part, 'label', scatter_dimension=0, tiled=True)  95.4 us
    all_to_all x1, blocking collectives, step(): recv = lax.all_to_all(send, 'doc', 0, 0, tiled=True)  50.3 us
    all_gather x1, waiting for transfers between devices, step(): rows = lax.all_gather(doc_embed, 'label', axis=0, tiled=True)  15.8 us
    all_to_all x1, starting transfers between devices, step(): lax.all_to_all(jnp.broadcast_to(ints[None], (n_label,) + ints.shape).resh...  13.2 us
    all_to_all x1, waiting for transfers between devices, step(): lax.all_to_all(jnp.broadcast_to(ints[None], (n_label,) + ints.shape).resh...  11.9 us
    all_to_all x1, starting transfers between devices, step(): lax.all_to_all(jnp.broadcast_to(centroids[None], (n_doc,) + centroids.sha...  7.82 us
    all_to_all x1, waiting for transfers between devices, step(): lax.all_to_all(jnp.broadcast_to(centroids[None], (n_doc,) + centroids.sha...  7.3 us
  transfers between devices with their start and end apart: 6, of which 4 were waited for; matrix products, arithmetic and copies ran while one was open for 7% of the time, Pallas kernels for 0%

profile of v1, /device:TPU:8, one launch (start us, length us, event | category | flops | bytes accessed | tf_op | source)
XLA Modules:
  0.0 259.0 jit_solution(16180941896402722525)
XLA Ops:
  8.9 1.3 gather_fusion
  10.7 1.1 reshape.131
  11.8 13.2 %all-to-all-start.1 = ((s32[32,1,1280]{2,1,0:T(1,128)}), s32[32,1,1280]{2,1,0:T(1,128)S(1)}, u32[]{:S(2)}, u32[]{:S(2)}) async-start(s32[32,1,1280]{2,1,0:T(1,128)} %reshape.131), calls=%async_computation.1 | async-start | bytes 327680 | tf_op jit(solution)/shard_map/all_to_all | solution.py:24
  24.9 11.9 %all-to-all-done.1 = s32[32,1,1280]{2,1,0:T(1,128)S(1)} async-done(((s32[32,1,1280]{2,1,0:T(1,128)}), s32[32,1,1280]{2,1,0:T(1,128)S(1)}, u32[]{:S(2)}, u32[]{:S(2)}) %all-to-all-start.1) | async-done | bytes 163872 | tf_op jit(solution)/shard_map/all_to_all | solution.py:24
  36.8 0.8 broadcast_in_dim.12
  37.6 7.8 %all-to-all-start = ((bf16[16,16,768]{2,1,0:T(8,128)(2,1)}), bf16[16,16,768]{2,1,0:T(8,128)(2,1)S(1)}, u32[]{:S(2)}, u32[]{:S(2)}) async-start(bf16[16,16,768]{2,1,0:T(8,128)(2,1)} %broadcast_in_dim.12), calls=%async_computation | async-start | bytes 786432 | tf_op jit(solution)/shard_map/all_to_all | solution.py:28
  47.0 1.0 reduce.1
  49.4 0.9 compare_reduce_fusion
  51.5 7.3 %all-to-all-done = bf16[16,16,768]{2,1,0:T(8,128)(2,1)S(1)} async-done(((bf16[16,16,768]{2,1,0:T(8,128)(2,1)}), bf16[16,16,768]{2,1,0:T(8,128)(2,1)S(1)}, u32[]{:S(2)}, u32[]{:S(2)}) %all-to-all-start) | async-done | bytes 393248 | tf_op jit(solution)/shard_map/all_to_all | solution.py:28
  58.8 15.8 %all-gather.2.cloned.1.call-done = bf16[1024,768]{1,0:T(8,128)(2,1)} async-done(((bf16[32,768]{1,0:T(8,128)(2,1)}), bf16[1024,768]{1,0:T(8,128)(2,1)}) %all-gather.2.cloned.1.call-update) | async-done | bytes 1572880 | tf_op jit(solution)/shard_map/all_gather | solution.py:40
  74.6 1.5 fusion.15
  76.1 1.6 copy.56
  77.7 3.4 %mul.45 = bf16[1024,8,128]{2,1,0:T(8,128)(2,1)S(1)} broadcast(bf16[1024,8]{1,0:T(8,128)(2,1)} %copy.56), dimensions={0,1} | broadcast | bytes 2113536 | tf_op jit(solution)/shard_map/mul | solution.py:51
  81.2 3.6 %bitcast_multiply_fusion = bf16[1024,1024]{1,0:T(8,128)(2,1)S(1)} fusion(bf16[128,8,8,128]{3,2,1,0:T(8,128)(2,1)S(1)} %bitcast.42, s32[1024]{0:T(1024)S(1)} %bitcast.49, s32[1024]{0:T(1024)S(1)} %bitcast.50, s32[1024]{0:T(1024)S(1)} %bitcast.51, s32[1024]{0:T(1024)S(1)} %copy-done.7, s32[1024]{0:T(1024)S(1)} %bitcast.48, ...), kind=kOutput, calls=%fused_computation.2 | convolution fusion | flops 1629487104 | bytes 7360512 | tf_op jit(solution)/shard_map/nd,ld->nl/dot_general | solution.py:45
  84.8 1.9 convolution_convert_fusion.1
  86.7 1.1 fusion.5
  88.8 50.3 %all_to_all.30 = bf16[16,72,768]{2,1,0:T(8,128)(2,1)S(1)} all-to-all(bf16[16,72,768]{2,1,0:T(8,128)(2,1)S(1)} %pad_maximum_fusion), channel_id=1, replica_groups=mesh['doc'=16,'label'=32] {'doc'}, dimensions={0} | all-to-all | bytes 3538944 | tf_op jit(solution)/shard_map/all_to_all | solution.py:80
  139.4 1.3 broadcast_in_dim.15
  140.7 4.3 %all-to-all-start.3 = ((bf16[16,64,768]{2,1,0:T(8,128)(2,1)}), bf16[16,64,768]{2,1,0:T(8,128)(2,1)}, u32[]{:S(2)}, u32[]{:S(2)}) async-start(bf16[16,64,768]{2,1,0:T(8,128)(2,1)} %broadcast_in_dim.15), calls=%async_computation.3 | async-start | bytes 3145728 | tf_op jit(solution)/shard_map/all_to_all | solution.py:92
  145.0 4.5 %convolution_convert_fusion = bf16[1024,768]{1,0:T(8,128)(2,1)} fusion(bf16[1024,1024]{1,0:T(8,128)(2,1)} %copy-done.12, bf16[1024,768]{1,0:T(8,128)(2,1)S(1)} %copy-done), kind=kOutput, calls=%fused_computation.4 | convolution fusion | flops 1611399168 | bytes 5242880 | tf_op jit(solution)/shard_map/dot_general | solution.py:56
  149.6 1.9 collective-permute-start
  151.6 95.4 %reduce-scatter.2.cloned.1.call-done = bf16[32,768]{1,0:T(8,128)(2,1)} async-done(((bf16[1024,768]{1,0:T(8,128)(2,1)}), bf16[32,768]{1,0:T(8,128)(2,1)}) %reduce-scatter.2.cloned.1.call-update) | async-done | bytes 49168 | tf_op jit(solution)/shard_map/reduce_scatter | solution.py:57
  247.0 1.8 fusion.6
  249.5 2.7 %broadcast_select_fusion = bf16[16,64,768]{2,1,0:T(8,128)(2,1)} fusion(bf16[16,64,768]{2,1,0:T(8,128)(2,1)} %all-to-all-done.3, pred[]{:T(512)S(6)} %ge.10), kind=kLoop, calls=%fused_computation.7 | loop fusion | flops 786432 | bytes 3145729 | tf_op jit(solution)/shard_map/jit(_where)/select_n | solution.py:93
  (59 shorter events, 8.2 us)
Async XLA Ops:
  7.2 74.0 %copy-start = (bf16[1024,768]{1,0:T(8,128)(2,1)S(1)}, bf16[1024,768]{1,0:T(8,128)(2,1)}, u32[]{:S(2)}) copy-start(bf16[1024,768]{1,0:T(8,128)(2,1)} %param.6) | copy-start | bytes 4718596
  7.2 1.6 copy-start.1
  7.2 67.4 %all-gather.2.cloned.1.call-start = ((), (), s32[]{:S(2)}) async-start(), calls=%async_computation.5 | async-start | bytes 1622016 | tf_op jit(solution)/shard_map/all_gather | solution.py:40
  8.8 1.5 copy-start.6
  8.8 28.0 %copy-start.5 = (bf16[16,768]{1,0:T(8,128)(2,1)S(1)}, bf16[16,768]{1,0:T(8,128)(2,1)}, u32[]{:S(2)}) copy-start(bf16[16,768]{1,0:T(8,128)(2,1)} %param.7) | copy-start | bytes 73732
  11.8 25.0 %all-to-all-start.1 = ((s32[32,1,1280]{2,1,0:T(1,128)}), s32[32,1,1280]{2,1,0:T(1,128)S(1)}, u32[]{:S(2)}, u32[]{:S(2)}) async-start(s32[32,1,1280]{2,1,0:T(1,128)} %reshape.131), calls=%async_computation.1 | async-start | bytes 327680 | tf_op jit(solution)/shard_map/all_to_all | solution.py:24
  37.6 21.2 %all-to-all-start = ((bf16[16,16,768]{2,1,0:T(8,128)(2,1)}), bf16[16,16,768]{2,1,0:T(8,128)(2,1)S(1)}, u32[]{:S(2)}, u32[]{:S(2)}) async-start(bf16[16,16,768]{2,1,0:T(8,128)(2,1)} %broadcast_in_dim.12), calls=%async_computation | async-start | bytes 786432 | tf_op jit(solution)/shard_map/all_to_all | solution.py:28
  58.8 27.9 %copy-start.3 = (bf16[16,16,768]{2,1,0:T(8,128)(2,1)}, bf16[16,16,768]{2,1,0:T(8,128)(2,1)S(1)}, u32[]{:S(2)}) copy-start(bf16[16,16,768]{2,1,0:T(8,128)(2,1)S(1)} %all-to-all-done) | copy-start | bytes 1179652
  74.6 6.5 %copy-start.2 = (bf16[1024,768]{1,0:T(8,128)(2,1)S(1)}, bf16[1024,768]{1,0:T(8,128)(2,1)}, u32[]{:S(2)}) copy-start(bf16[1024,768]{1,0:T(8,128)(2,1)} %all-gather.2.cloned.1.call-done) | copy-start | bytes 4718596
  77.7 3.5 %copy-start.7 = (s32[1024]{0:T(1024)S(1)}, s32[1024]{0:T(1024)}, u32[]{:S(2)}) copy-start(s32[1024]{0:T(1024)} %add_bitcast_fusion) | copy-start | bytes 12292
  77.7 3.5 %copy-start.8 = (s32[1024,1]{0,1:T(1,128)S(1)}, s32[1024,1]{0,1:T(1,128)}, u32[]{:S(2)}) copy-start(s32[1024,1]{0,1:T(1,128)} %get-tuple-element.15) | copy-start | bytes 12292
  77.7 3.5 %copy-start.9 = (s32[1024,1]{0,1:T(1,128)S(1)}, s32[1024,1]{0,1:T(1,128)}, u32[]{:S(2)}) copy-start(s32[1024,1]{0,1:T(1,128)} %get-tuple-element.16) | copy-start | bytes 12292
  77.7 3.5 %copy-start.10 = (s32[1024,1]{0,1:T(1,128)S(1)}, s32[1024,1]{0,1:T(1,128)}, u32[]{:S(2)}) copy-start(s32[1024,1]{0,1:T(1,128)} %get-tuple-element.17) | copy-start | bytes 12292
  77.7 3.5 %copy-start.11 = (s32[1024,1]{0,1:T(1,128)S(1)}, s32[1024,1]{0,1:T(1,128)}, u32[]{:S(2)}) copy-start(s32[1024,1]{0,1:T(1,128)} %get-tuple-element.18) | copy-start | bytes 12292
  84.8 1.9 copy-start.12
  87.9 0.8 copy-start.4
  140.7 108.8 %all-to-all-start.3 = ((bf16[16,64,768]{2,1,0:T(8,128)(2,1)}), bf16[16,64,768]{2,1,0:T(8,128)(2,1)}, u32[]{:S(2)}, u32[]{:S(2)}) async-start(bf16[16,64,768]{2,1,0:T(8,128)(2,1)} %broadcast_in_dim.15), calls=%async_computation.3 | async-start | bytes 3145728 | tf_op jit(solution)/shard_map/all_to_all | solution.py:92
  145.0 102.0 %reduce-scatter.2.cloned.1.call-start = ((), (), s32[]{:S(2)}) async-start(), calls=%async_computation.6 | async-start | bytes 1622016 | tf_op jit(solution)/shard_map/reduce_scatter | solution.py:57
  149.6 99.2 %collective-permute-start = (f32[8,768]{1,0:T(8,128)S(1)}, f32[8,768]{1,0:T(8,128)S(1)}, u32[]{:S(2)}, u32[]{:S(2)}) collective-permute-start(f32[8,768]{1,0:T(8,128)S(1)} %convert_reduce_fusion), channel_id=1, source_target_pairs={{0,1},{1,0},{2,3},{3,2},{4,5},{5,4},{6,7},{7,6},{8,9},{9,8},{10,11... | collective-permute-start | bytes 73736 | tf_op jit(solution)/shard_map/ppermute | solution.py:85
Sparse Core Ops, SparseCore 0:
  11.1 63.4 all-gather.1
  150.2 96.7 reduce-scatter.1
